TPU v7x, 512 devices: a whole 4x4x16 slice. The times are simulated.
512 devices in a mesh: ctx: 16 (over z), ep: 32 (over y, x, core).
Axes of the slice: x: 4, y: 4, z: 16, core: 2. Of those that a mesh axis runs over, the one named last changes fastest.
Arguments:
- query_act: bfloat16 [2048, 8192], P('ctx', 'ep'), may hold values from -6 to 6
- key_act: bfloat16 [2048, 8192], P('ctx', 'ep'), may hold values from -6 to 6
- value_act: bfloat16 [2048, 8192], P('ctx', 'ep'), may hold values from -6 to 6
- state_init: float32 [64, 128, 128], P('ep'), may hold values from -128 to 128
- head_gain: float32 [8192], P('ep'), may hold values from 0.25 to 1.75
- out_weight: bfloat16 [8192, 3072], P('ctx', 'ep'), may hold values from -0.0625 to 0.0625
- stream_in: bfloat16 [2048, 3072], P('ctx', 'ep'), may hold values from -150 to 150
- model_gain: float32 [3072], replicated, may hold values from 0.25 to 1.75
- expert_ids: int32 [2048, 2], P('ctx'), may hold values from 0 to 15, as said below
- expert_slots: int32 [2048, 2], P('ctx'), may hold values from 0 to 19, as said below
- route_gates: float32 [2048, 2], P('ctx'), may hold values from 0.2 to 1
- gate_weight: bfloat16 [32, 3072, 3072], P('ep', 'ctx'), may hold values from -0.109375 to 0.109375
- up_weight: bfloat16 [32, 3072, 3072], P('ep', 'ctx'), may hold values from -0.109375 to 0.109375
- down_weight: bfloat16 [32, 3072, 3072], P('ep', 'ctx'), may hold values from -0.078125 to 0.078125
- out_grad: bfloat16 [2048, 3072], P('ctx', 'ep'), may hold values from -6 to 6
Outputs:
- layer_out: bfloat16 [2048, 3072], P('ctx', 'ep')
- grad_query: bfloat16 [2048, 8192], P('ctx', 'ep')
- grad_key: bfloat16 [2048, 8192], P('ctx', 'ep')
- grad_value: bfloat16 [2048, 8192], P('ctx', 'ep')
- grad_state: float32 [64, 128, 128], P('ep')
- grad_stream: bfloat16 [2048, 3072], P('ctx', 'ep')
Inputs may be any that keep to these rules, and one draw needn't show every extreme that they name: `expert_ids`: within each block of 128 tokens a token's two experts differ; the tokens naming expert e hold the slots 0 to n - 1 of e once each, n being their number; no expert is named by more than 20 tokens of a block, and in every block some expert by exactly 20. `expert_slots`: see expert_ids.
All inputs are finite; a program needn't handle non-finite values.
Results may differ from a plain program's by a relative error of at most 0.02.
Values may be sent and summed in bfloat16 or wider, within the bound.
No kernel may reach another device: no remote copies, remote signals or barrier semaphores. Data moves between devices by JAX's collectives and lax.ppermute only.
A program may use at most 64 MiB of HBM per device.

v0:
```python
import jax
import jax.numpy as jnp
from jax import lax
from jax.sharding import PartitionSpec as P


def butterfly_sums(value, axis, backward):
    count = lax.axis_size(axis)
    place = lax.axis_index(axis)
    total = value
    carried = jnp.zeros_like(value)
    step = 1
    while step < count:
        other = lax.ppermute(total, axis, [(i, i ^ step) for i in range(count)])
        upper = place & step != 0
        take = jnp.logical_not(upper) if backward else upper
        carried = carried + jnp.where(take, other, jnp.zeros_like(other))
        total = total + other
        step *= 2
    return (carried, total)


def gather_blocks(value, axis):
    count = lax.axis_size(axis)
    spread = jnp.broadcast_to(value[None], (count,) + value.shape)
    return lax.all_to_all(spread, axis, 0, 0, tiled=True)


def scatter_sum(values, axis):
    count = lax.axis_size(axis)
    rows, width = values[0].shape
    block = rows // count
    joined = jnp.concatenate([value.reshape(count, block, width) for value in values], 1)
    part = lax.psum_scatter(joined, axis, scatter_dimension=0, tiled=True)
    return [part[0, i * block : (i + 1) * block] for i in range(len(values))]


def head_normalize(attended, gain):
    factor = lax.rsqrt(jnp.mean(attended * attended, -1, keepdims=True) + 1e-06)
    return attended * factor * gain


def contract_last(left, right):
    return lax.dot_general(
        left, right, (((1,), (1,)), ((), ())), preferred_element_type=jnp.float32
    )


def local(
    query_act,
    key_act,
    value_act,
    state_init,
    head_gain,
    out_weight,
    stream_in,
    model_gain,
    expert_ids,
    expert_slots,
    route_gates,
    gate_weight,
    up_weight,
    down_weight,
    out_grad,
):
    f32 = jnp.float32
    high = lax.Precision.HIGHEST
    ep_count = lax.axis_size("ep")
    expert_count = ep_count // 2
    my_ep = lax.axis_index("ep")
    tokens_here = query_act.shape[0]
    head_count = state_init.shape[0]
    head_size = state_init.shape[1]
    model_width = model_gain.shape[0]
    columns = stream_in.shape[1]
    capacity = 5 * tokens_here // (2 * expert_count)
    w_cols = lax.all_gather(out_weight, "ctx", axis=0, tiled=True)
    query3 = query_act.reshape(tokens_here, head_count, head_size)
    key3 = key_act.reshape(tokens_here, head_count, head_size)
    value3 = value_act.reshape(tokens_here, head_count, head_size)
    kv_own = jnp.einsum("thd,the->hde", key3, value3, preferred_element_type=f32)
    before, _ = butterfly_sums(kv_own, "ctx", False)
    prefix = state_init + before
    causal = jnp.arange(tokens_here)[:, None] >= jnp.arange(tokens_here)[None, :]
    scores = jnp.einsum("thd,shd->hts", query3, key3, preferred_element_type=f32)
    scores_bf = jnp.where(causal[None], scores, 0.0).astype(jnp.bfloat16)
    inside = jnp.einsum("hts,she->the", scores_bf, value3, preferred_element_type=f32)
    from_state = jnp.einsum("thd,hde->the", query3.astype(f32), prefix, precision=high)
    attended = from_state + inside
    gain_heads = head_gain.reshape(head_count, head_size)
    normed_heads = (
        head_normalize(attended, gain_heads)
        .astype(jnp.bfloat16)
        .reshape(tokens_here, head_count * head_size)
    )
    w_blocks = w_cols.reshape(ep_count, head_count * head_size, columns)
    attn_proj = jnp.einsum(
        "ith,ihf->tf", gather_blocks(normed_heads, "ep"), w_blocks, preferred_element_type=f32
    )
    stream = (stream_in.astype(f32) + attn_proj).astype(jnp.bfloat16)
    stream_f = stream.astype(f32)
    gain_cols = lax.dynamic_slice_in_dim(model_gain, my_ep * columns, columns, 0)
    dest_expert = jnp.arange(ep_count) % expert_count
    slot_iota = jnp.arange(capacity)
    hits = (expert_ids[:, :, None, None] == dest_expert[None, None, :, None]) & (
        expert_slots[:, :, None, None] == slot_iota[None, None, None, :]
    )
    hits_f = hits.astype(f32)
    dest_picks = jnp.sum(hits_f, 1).reshape(tokens_here, ep_count * capacity)
    dest_weights = jnp.sum(hits_f * route_gates[:, :, None, None], 1).reshape(
        tokens_here, ep_count * capacity
    )
    picked = jnp.dot(dest_picks.T.astype(jnp.bfloat16), stream, preferred_element_type=f32).astype(
        jnp.bfloat16
    )
    arrived = lax.all_to_all(picked.reshape(ep_count, capacity, columns), "ep", 0, 0, tiled=True)
    slot_rows = arrived.transpose(1, 0, 2).reshape(capacity, model_width).astype(f32)
    slot_scale = lax.rsqrt(jnp.mean(slot_rows * slot_rows, -1, keepdims=True) + 1e-05)
    expert_in = (slot_rows * slot_scale * model_gain).astype(jnp.bfloat16)
    w_gate = gate_weight[0]
    w_up = up_weight[0]
    w_down = down_weight[0]
    hidden_block = w_gate.shape[0]
    w_rows = lax.all_to_all(w_blocks, "ep", 0, 0, tiled=True)
    portion = lax.all_gather(expert_in, "ctx", axis=0, tiled=True)
    square_sums = jnp.sum(gather_blocks(jnp.sum(stream_f * stream_f, -1, keepdims=True), "ep"), 0)
    row_scale = lax.rsqrt(square_sums / model_width + 1e-05)
    projected = jnp.concatenate([contract_last(portion, w_gate), contract_last(portion, w_up)], 1)
    pre_gate = projected[:, :hidden_block]
    pre_up = projected[:, hidden_block:]
    gate_sig = jax.nn.sigmoid(pre_gate)
    activated = (pre_gate * gate_sig * pre_up).astype(jnp.bfloat16)
    out_terms = jnp.dot(activated, w_down, preferred_element_type=f32).astype(jnp.bfloat16)
    grad_out = out_grad.astype(f32)
    grad_send = jnp.dot(dest_weights.T, grad_out, precision=high).astype(jnp.bfloat16)
    grad_in = lax.all_to_all(grad_send, "ep", split_axis=0, concat_axis=1, tiled=True)
    grad_rows_all = lax.all_gather(grad_in, "ctx", axis=0, tiled=True)
    portion, w_rows, square_sums, grad_rows_all = lax.optimization_barrier(
        (portion, w_rows, square_sums, grad_rows_all)
    )
    row_scale = lax.rsqrt(square_sums / model_width + 1e-05)
    grad_act = contract_last(grad_rows_all, w_down)
    grad_gate_pre = (grad_act * pre_up * gate_sig * (1.0 + pre_gate * (1.0 - gate_sig))).astype(
        jnp.bfloat16
    )
    grad_up_pre = (grad_act * pre_gate * gate_sig).astype(jnp.bfloat16)
    grad_terms = (
        jnp.dot(grad_gate_pre, w_gate, preferred_element_type=f32)
        + jnp.dot(grad_up_pre, w_up, preferred_element_type=f32)
    ).astype(jnp.bfloat16)
    half_out, grad_half = scatter_sum([out_terms, grad_terms], "ctx")
    slot_inner = jnp.sum(slot_rows * model_gain * grad_half.astype(f32), -1, keepdims=True)
    inner_hi = slot_inner.astype(jnp.bfloat16)
    inner_lo = (slot_inner - inner_hi.astype(f32)).astype(jnp.bfloat16)
    inner_pair = jnp.broadcast_to(
        jnp.concatenate([inner_hi, inner_lo], -1)[:, None, :], (capacity, ep_count, 2)
    )
    payload = jnp.concatenate([grad_half.reshape(capacity, ep_count, columns), inner_pair], -1)
    grad_back = lax.all_to_all(payload, "ep", split_axis=1, concat_axis=0, tiled=True)
    grad_back = grad_back.reshape(ep_count * capacity, columns + 2).astype(f32)
    grad_model_in = jnp.dot(dest_picks, grad_back[:, :columns], precision=high)
    scaled_grad = grad_model_in * gain_cols
    inner_sum = jnp.dot(
        dest_picks,
        grad_back[:, columns : columns + 1] + grad_back[:, columns + 1 :],
        precision=high,
    )
    grad_stream = (
        grad_out + row_scale * scaled_grad - stream_f * row_scale**3 * inner_sum / model_width
    ).astype(jnp.bfloat16)
    grad_heads = jnp.einsum(
        "itf,ihf->th", gather_blocks(grad_stream, "ep"), w_rows, preferred_element_type=f32
    )
    head_pull = jax.vjp(lambda value: head_normalize(value, gain_heads), attended)[1]
    grad_attended = head_pull(grad_heads.reshape(tokens_here, head_count, head_size))[0].astype(
        jnp.bfloat16
    )
    state_part = jnp.einsum("thd,the->hde", query3, grad_attended, preferred_element_type=f32)
    half_out, state_part = lax.optimization_barrier((half_out, state_part))
    returned = lax.all_to_all(half_out, "ep", split_axis=1, concat_axis=0, tiled=True)
    expert_mix = jnp.dot(dest_weights, returned.astype(f32), precision=high)
    layer_out = (stream_f + expert_mix).astype(jnp.bfloat16)
    later_sum, state_total = butterfly_sums(state_part, "ctx", True)
    grad_scores = jnp.einsum("the,she->hts", grad_attended, value3, preferred_element_type=f32)
    grad_masked = jnp.where(causal[None], grad_scores, 0.0).astype(jnp.bfloat16)
    grad_att_f = grad_attended.astype(f32)
    grad_query = jnp.einsum("the,hde->thd", grad_att_f, prefix, precision=high) + jnp.einsum(
        "hts,shd->thd", grad_masked, key3, preferred_element_type=f32
    )
    grad_key = jnp.einsum(
        "the,hde->thd", value3.astype(f32), later_sum, precision=high
    ) + jnp.einsum("hts,thd->shd", grad_masked, query3, preferred_element_type=f32)
    grad_value = jnp.einsum(
        "thd,hde->the", key3.astype(f32), later_sum, precision=high
    ) + jnp.einsum("hts,the->she", scores_bf, grad_attended, preferred_element_type=f32)
    flat_shape = (tokens_here, head_count * head_size)
    return (
        layer_out,
        grad_query.astype(jnp.bfloat16).reshape(flat_shape),
        grad_key.astype(jnp.bfloat16).reshape(flat_shape),
        grad_value.astype(jnp.bfloat16).reshape(flat_shape),
        state_total,
        grad_stream,
    )


def solution(mesh):
    return jax.shard_map(
        local,
        mesh=mesh,
        in_specs=(
            P("ctx", "ep"),
            P("ctx", "ep"),
            P("ctx", "ep"),
            P("ep", None, None),
            P("ep"),
            P("ctx", "ep"),
            P("ctx", "ep"),
            P(),
            P("ctx", None),
            P("ctx", None),
            P("ctx", None),
            P("ep", "ctx", None),
            P("ep", "ctx", None),
            P("ep", "ctx", None),
            P("ctx", "ep"),
        ),
        out_specs=(
            P("ctx", "ep"),
            P("ctx", "ep"),
            P("ctx", "ep"),
            P("ctx", "ep"),
            P("ep", None, None),
            P("ctx", "ep"),
        ),
        check_vma=False,
    )
```

profile of v0, /device:TPU:1, one launch (start us, length us, event | category | flops | bytes accessed | tf_op | source)
XLA Modules:
  0.0 460.4 jit_solution(4378941329821075117)
XLA Ops:
  7.9 1.0 copy.262
  8.9 1.0 fusion.47
  9.9 4.4 collective-permute-start
  15.0 0.8 broadcast_compare_fusion
  15.7 0.9 fusion.28
  16.7 0.7 copy-done.5
  17.7 4.9 %collective-permute-start.1 = (f32[2,128,128]{2,1,0:T(8,128)S(1)}, f32[2,128,128]{2,1,0:T(8,128)S(1)}, u32[]{:S(2)}, u32[]{:S(2)}) collective-permute-start(f32[2,128,128]{2,1,0:T(8,128)S(1)} %add.116), channel_id=1, source_target_pairs={{0,64},{32,96},{64,0},{96,32},{128,192},{160,224},{192,128},{224,1... | collective-permute-start | bytes 393224 | tf_op jit(solution)/shard_map/ppermute | solution.py:14
  23.1 0.8 all_to_all.56
  23.9 8.4 %all-to-all-start.4 = ((bf16[32,20,96]{2,1,0:T(8,128)(2,1)}), bf16[32,20,96]{2,1,0:T(8,128)(2,1)S(1)}, u32[]{:S(2)}, u32[]{:S(2)}) async-start(bf16[32,20,96]{2,1,0:T(8,128)(2,1)} %all_to_all.56), calls=%async_computation.4 | async-start | bytes 393216 | tf_op jit(solution)/shard_map/all_to_all | solution.py:136
  32.5 8.8 %collective-permute-start.2 = (f32[2,128,128]{2,1,0:T(8,128)S(1)}, f32[2,128,128]{2,1,0:T(8,128)S(1)}, u32[]{:S(2)}, u32[]{:S(2)}) collective-permute-start(f32[2,128,128]{2,1,0:T(8,128)S(1)} %add.118), channel_id=1, source_target_pairs={{0,128},{32,160},{64,192},{96,224},{128,0},{160,32},{192,64},{224,... | collective-permute-start | bytes 393224 | tf_op jit(solution)/shard_map/ppermute | solution.py:14
  41.6 14.2 %collective-permute-done.2 = f32[2,128,128]{2,1,0:T(8,128)S(1)} collective-permute-done((f32[2,128,128]{2,1,0:T(8,128)S(1)}, f32[2,128,128]{2,1,0:T(8,128)S(1)}, u32[]{:S(2)}, u32[]{:S(2)}) %collective-permute-start.2) | collective-permute-done | bytes 131104 | tf_op jit(solution)/shard_map/ppermute | solution.py:14
  55.8 11.5 %collective-permute-start.3 = (f32[2,128,128]{2,1,0:T(8,128)S(1)}, f32[2,128,128]{2,1,0:T(8,128)S(1)}, u32[]{:S(2)}, u32[]{:S(2)}) collective-permute-start(f32[2,128,128]{2,1,0:T(8,128)S(1)} %add.120), channel_id=1, source_target_pairs={{0,256},{32,288},{64,320},{96,352},{128,384},{160,416},{192,448},{... | collective-permute-start | bytes 393224 | tf_op jit(solution)/shard_map/ppermute | solution.py:14
  67.5 4.1 collective-permute-done.3
  72.9 1.6 broadcast_in_dim.30
  74.5 14.6 %all-to-all-start = ((bf16[32,128,256]{2,1,0:T(8,128)(2,1)}), bf16[32,128,256]{2,1,0:T(8,128)(2,1)}, u32[]{:S(2)}, u32[]{:S(2)}) async-start(bf16[32,128,256]{2,1,0:T(8,128)(2,1)} %broadcast_in_dim.30), calls=%async_computation | async-start | bytes 4194304 | tf_op jit(solution)/shard_map/all_to_all | solution.py:26
  89.3 0.9 reshape.187
  90.5 27.4 %all-to-all-done = bf16[32,128,256]{2,1,0:T(8,128)(2,1)} async-done(((bf16[32,128,256]{2,1,0:T(8,128)(2,1)}), bf16[32,128,256]{2,1,0:T(8,128)(2,1)}, u32[]{:S(2)}, u32[]{:S(2)}) %all-to-all-start) | async-done | bytes 2097184 | tf_op jit(solution)/shard_map/all_to_all | solution.py:26
  117.9 3.4 fusion.51
  121.7 12.8 %all_to_all.75 = bf16[32,20,96]{2,1,0:T(8,128)(2,1)S(1)} all-to-all(bf16[32,20,96]{2,1,0:T(8,128)(2,1)S(1)} %reshape.174), channel_id=1, replica_groups=mesh['ctx'=16,'ep'=32] {'ep'}, dimensions={0} | all-to-all | bytes 245760 | tf_op jit(solution)/shard_map/all_to_all | solution.py:116
  134.6 0.8 copy.196
  135.4 1.9 reshape.184
  137.5 1.7 fusion.37
  139.3 1.3 broadcast_in_dim.31
  140.5 3.8 all-to-all-start.3
  144.3 1.4 copy.265
  145.8 5.4 %all-to-all-done.3 = f32[32,128,1]{1,2,0:T(1,128)S(1)} async-done(((f32[32,128,1]{1,2,0:T(1,128)}), f32[32,128,1]{1,2,0:T(1,128)S(1)}, u32[]{:S(2)}, u32[]{:S(2)}) %all-to-all-start.3) | async-done | bytes 16416 | tf_op jit(solution)/shard_map/all_to_all | solution.py:26
  151.2 4.3 all-to-all-start.2
  155.8 8.7 %all-gather.10.cloned.1.call-done = bf16[16,20,3072]{2,1,0:T(8,128)(2,1)} async-done(((bf16[1,20,3072]{2,1,0:T(8,128)(2,1)}), bf16[16,20,3072]{2,1,0:T(8,128)(2,1)}) %all-gather.10.cloned.1.call-update) | async-done | bytes 1966096 | tf_op jit(solution)/shard_map/all_gather | solution.py:137
  164.5 4.0 reshape.188
  168.5 68.1 %all-gather.8.cloned.1.call-done = bf16[16,20,3072]{2,1,0:T(8,128)(2,1)} async-done(((bf16[1,20,3072]{2,1,0:T(8,128)(2,1)}), bf16[16,20,3072]{2,1,0:T(8,128)(2,1)}) %all-gather.8.cloned.1.call-update) | async-done | bytes 1966096 | tf_op jit(solution)/shard_map/all_gather | solution.py:125
  236.5 3.9 reshape.186
  240.5 3.4 fusion.5
  243.9 0.9 fusion.9
  245.5 0.9 fusion.1
  246.4 0.7 convolution_convert_fusion
  247.2 0.8 fusion.7
  248.4 2.0 fusion
  250.5 3.9 reshape.177
  254.4 2.1 reshape.175
  256.5 5.2 %pad_maximum_fusion = bf16[16,40,3072]{2,1,0:T(8,128)(2,1)} fusion(bf16[16,20,3072]{2,1,0:T(8,128)(2,1)} %reshape.177, bf16[16,20,3072]{2,1,0:T(8,128)(2,1)} %reshape.175), kind=kLoop, calls=%fused_computation.3 | loop fusion | flops 7864320 | bytes 7864320 | tf_op jit(solution)/shard_map/concatenate | solution.py:33
  261.9 75.8 %reduce-scatter.2.cloned.1.call-done = bf16[1,40,3072]{2,1,0:T(8,128)(2,1)} async-done(((bf16[16,40,3072]{2,1,0:T(8,128)(2,1)}), bf16[1,40,3072]{2,1,0:T(8,128)(2,1)}) %reduce-scatter.2.cloned.1.call-update) | async-done | bytes 245776 | tf_op jit(solution)/shard_map/reduce_scatter | solution.py:34
  337.7 1.7 fusion.65
  340.0 0.7 copy.203
  340.8 18.3 %all-to-all-start.5 = ((bf16[20,32,98]{2,0,1:T(8,128)(2,1)}), bf16[20,32,98]{2,0,1:T(8,128)(2,1)S(1)}, u32[]{:S(2)}, u32[]{:S(2)}) async-start(bf16[20,32,98]{2,0,1:T(8,128)(2,1)} %copy.203), calls=%async_computation.6 | async-start | bytes 393216 | tf_op jit(solution)/shard_map/all_to_all | solution.py:159
  359.1 8.2 %all-to-all-done.5 = bf16[20,32,98]{2,0,1:T(8,128)(2,1)S(1)} async-done(((bf16[20,32,98]{2,0,1:T(8,128)(2,1)}), bf16[20,32,98]{2,0,1:T(8,128)(2,1)S(1)}, u32[]{:S(2)}, u32[]{:S(2)}) %all-to-all-start.5) | async-done | bytes 125472 | tf_op jit(solution)/shard_map/all_to_all | solution.py:159
  368.8 1.3 fusion.25
  370.1 1.0 broadcast_in_dim.33
  371.1 3.8 all-to-all-start.6
  374.9 14.3 %all-to-all-done.6 = bf16[32,128,96]{1,2,0:T(8,128)(2,1)S(1)} async-done(((bf16[32,128,96]{1,2,0:T(8,128)(2,1)}), bf16[32,128,96]{1,2,0:T(8,128)(2,1)S(1)}, u32[]{:S(2)}, u32[]{:S(2)}) %all-to-all-start.6) | async-done | bytes 786464 | tf_op jit(solution)/shard_map/all_to_all | solution.py:26
  389.2 0.7 fusion.67
  390.7 2.6 collective-permute-start.4
  393.7 0.7 copy.217
  394.7 0.7 copy.207
  395.4 4.5 all-to-all-start.7
  399.9 4.3 collective-permute-start.5
  404.4 6.1 %collective-permute-done.5 = f32[2,128,128]{2,1,0:T(8,128)S(1)} collective-permute-done((f32[2,128,128]{2,1,0:T(8,128)S(1)}, f32[2,128,128]{2,1,0:T(8,128)S(1)}, u32[]{:S(2)}, u32[]{:S(2)}) %collective-permute-start.5) | collective-permute-done | bytes 131104 | tf_op jit(solution)/shard_map/ppermute | solution.py:14
  410.6 6.0 %collective-permute-start.6 = (f32[2,128,128]{2,1,0:T(8,128)S(1)}, f32[2,128,128]{2,1,0:T(8,128)S(1)}, u32[]{:S(2)}, u32[]{:S(2)}) collective-permute-start(f32[2,128,128]{2,1,0:T(8,128)S(1)} %add.140), channel_id=1, source_target_pairs={{0,128},{32,160},{64,192},{96,224},{128,0},{160,32},{192,64},{224,... | collective-permute-start | bytes 393224 | tf_op jit(solution)/shard_map/ppermute | solution.py:14
  416.8 11.7 %collective-permute-done.6 = f32[2,128,128]{2,1,0:T(8,128)S(1)} collective-permute-done((f32[2,128,128]{2,1,0:T(8,128)S(1)}, f32[2,128,128]{2,1,0:T(8,128)S(1)}, u32[]{:S(2)}, u32[]{:S(2)}) %collective-permute-start.6) | collective-permute-done | bytes 131104 | tf_op jit(solution)/shard_map/ppermute | solution.py:14
  428.5 8.4 %collective-permute-start.7 = (f32[2,128,128]{2,1,0:T(8,128)S(1)}, f32[2,128,128]{2,1,0:T(8,128)S(1)}, u32[]{:S(2)}, u32[]{:S(2)}) collective-permute-start(f32[2,128,128]{2,1,0:T(8,128)S(1)} %add.142), channel_id=1, source_target_pairs={{0,256},{32,288},{64,320},{96,352},{128,384},{160,416},{192,448},{... | collective-permute-start | bytes 393224 | tf_op jit(solution)/shard_map/ppermute | solution.py:14
  437.0 1.0 fusion.26
  438.0 13.2 %collective-permute-done.7 = f32[2,128,128]{2,1,0:T(8,128)S(1)} collective-permute-done((f32[2,128,128]{2,1,0:T(8,128)S(1)}, f32[2,128,128]{2,1,0:T(8,128)S(1)}, u32[]{:S(2)}, u32[]{:S(2)}) %collective-permute-start.7) | collective-permute-done | bytes 131104 | tf_op jit(solution)/shard_map/ppermute | solution.py:14
  451.2 0.7 fusion.66
  452.2 0.7 copy.219
  453.2 0.7 copy.218
  (161 shorter events, 10.8 us)
Async XLA Ops:
  7.2 237.7 %copy-start = (bf16[1,192,3072]{2,1,0:T(8,128)(2,1)S(1)}, bf16[1,192,3072]{2,1,0:T(8,128)(2,1)}, u32[]{:S(2)}) copy-start(bf16[1,192,3072]{2,1,0:T(8,128)(2,1)} %param.28) | copy-start | bytes 3538948
  7.2 15.4 %copy-start.34 = (bf16[128,96]{0,1:T(8,128)(2,1)S(1)}, bf16[128,96]{0,1:T(8,128)(2,1)}, u32[]{:S(2)}) copy-start(bf16[128,96]{0,1:T(8,128)(2,1)} %param.29) | copy-start | bytes 73732
  7.2 110.7 %all-gather.6.cloned.1.call-start = ((), (), s32[]{:S(2)}) async-start(), calls=%async_computation.9 | async-start | bytes 1671168 | tf_op jit(solution)/shard_map/all_gather | solution.py:77
  8.9 7.8 %copy-start.21 = (bf16[128,256]{0,1:T(8,128)(2,1)}, bf16[128,256]{0,1:T(8,128)(2,1)S(1)}, u32[]{:S(2)}) copy-start(bf16[128,256]{0,1:T(8,128)(2,1)S(1)} %copy.262) | copy-start | bytes 196612
  9.9 7.8 %collective-permute-start = (f32[2,128,128]{2,1,0:T(8,128)S(1)}, f32[2,128,128]{2,1,0:T(8,128)S(1)}, u32[]{:S(2)}, u32[]{:S(2)}) collective-permute-start(f32[2,128,128]{2,1,0:T(8,128)S(1)} %fusion.47), channel_id=1, source_target_pairs={{0,32},{32,0},{64,96},{96,64},{128,160},{160,128},{192,224},{224,1... | collective-permute-start | bytes 393224 | tf_op jit(solution)/shard_map/ppermute | solution.py:14
  15.7 16.6 %copy-start.35 = (bf16[128,256]{1,0:T(8,128)(2,1)S(1)}, bf16[128,256]{1,0:T(8,128)(2,1)}, u32[]{:S(2)}) copy-start(bf16[128,256]{1,0:T(8,128)(2,1)} %param.15) | copy-start | bytes 196612
  16.7 0.7 copy-start.5
  16.7 24.7 %copy-start.26 = (bf16[128,256]{1,0:T(8,128)(2,1)S(1)}, bf16[128,256]{1,0:T(8,128)(2,1)}, u32[]{:S(2)}) copy-start(bf16[128,256]{1,0:T(8,128)(2,1)} %param.16) | copy-start | bytes 196612
  17.6 49.7 %copy-start.23 = (bf16[128,256]{1,0:T(8,128)(2,1)S(1)}, bf16[128,256]{1,0:T(8,128)(2,1)}, u32[]{:S(2)}) copy-start(bf16[128,256]{1,0:T(8,128)(2,1)} %param.17) | copy-start | bytes 196612
  17.6 54.0 %copy-start.32 = (f32[2,128,128]{2,1,0:T(8,128)S(1)}, f32[2,128,128]{2,1,0:T(8,128)}, u32[]{:S(2)}) copy-start(f32[2,128,128]{2,1,0:T(8,128)} %param.18) | copy-start | bytes 393220
  17.7 14.8 %collective-permute-start.1 = (f32[2,128,128]{2,1,0:T(8,128)S(1)}, f32[2,128,128]{2,1,0:T(8,128)S(1)}, u32[]{:S(2)}, u32[]{:S(2)}) collective-permute-start(f32[2,128,128]{2,1,0:T(8,128)S(1)} %add.116), channel_id=1, source_target_pairs={{0,64},{32,96},{64,0},{96,32},{128,192},{160,224},{192,128},{224,1... | collective-permute-start | bytes 393224 | tf_op jit(solution)/shard_map/ppermute | solution.py:14
  23.0 49.7 %copy-start.37 = (f32[256]{0:T(256)S(1)}, f32[256]{0:T(256)}, u32[]{:S(2)}) copy-start(f32[256]{0:T(256)} %param.19) | copy-start | bytes 3076
  23.9 49.0 %all-to-all-start.4 = ((bf16[32,20,96]{2,1,0:T(8,128)(2,1)}), bf16[32,20,96]{2,1,0:T(8,128)(2,1)S(1)}, u32[]{:S(2)}, u32[]{:S(2)}) async-start(bf16[32,20,96]{2,1,0:T(8,128)(2,1)} %all_to_all.56), calls=%async_computation.4 | async-start | bytes 393216 | tf_op jit(solution)/shard_map/all_to_all | solution.py:136
  32.4 42.1 %copy-start.17 = (bf16[128,256]{0,1:T(8,128)(2,1)}, bf16[128,256]{0,1:T(8,128)(2,1)S(1)}, u32[]{:S(2)}) copy-start(bf16[128,256]{0,1:T(8,128)(2,1)S(1)} %copy.229) | copy-start | bytes 196612
  32.5 23.3 %collective-permute-start.2 = (f32[2,128,128]{2,1,0:T(8,128)S(1)}, f32[2,128,128]{2,1,0:T(8,128)S(1)}, u32[]{:S(2)}, u32[]{:S(2)}) collective-permute-start(f32[2,128,128]{2,1,0:T(8,128)S(1)} %add.118), channel_id=1, source_target_pairs={{0,128},{32,160},{64,192},{96,224},{128,0},{160,32},{192,64},{224,... | collective-permute-start | bytes 393224 | tf_op jit(solution)/shard_map/ppermute | solution.py:14
  41.6 33.0 %copy-start.28 = (bf16[2,128,128]{2,1,0:T(8,128)(2,1)}, bf16[2,128,128]{2,1,0:T(8,128)(2,1)S(1)}, u32[]{:S(2)}) copy-start(bf16[2,128,128]{2,1,0:T(8,128)(2,1)S(1)} %fusion.14) | copy-start | bytes 196612
  55.8 15.8 %collective-permute-start.3 = (f32[2,128,128]{2,1,0:T(8,128)S(1)}, f32[2,128,128]{2,1,0:T(8,128)S(1)}, u32[]{:S(2)}, u32[]{:S(2)}) collective-permute-start(f32[2,128,128]{2,1,0:T(8,128)S(1)} %add.120), channel_id=1, source_target_pairs={{0,256},{32,288},{64,320},{96,352},{128,384},{160,416},{192,448},{... | collective-permute-start | bytes 393224 | tf_op jit(solution)/shard_map/ppermute | solution.py:14
  71.7 1.1 copy-start.13
  72.0 0.7 copy-start.7
  72.0 2.5 copy-start.41
  72.1 2.5 copy-start.39
  74.5 43.4 %all-to-all-start = ((bf16[32,128,256]{2,1,0:T(8,128)(2,1)}), bf16[32,128,256]{2,1,0:T(8,128)(2,1)}, u32[]{:S(2)}, u32[]{:S(2)}) async-start(bf16[32,128,256]{2,1,0:T(8,128)(2,1)} %broadcast_in_dim.30), calls=%async_computation | async-start | bytes 4194304 | tf_op jit(solution)/shard_map/all_to_all | solution.py:26
  89.2 28.7 %copy-start.43 = (bf16[128,96]{0,1:T(8,128)(2,1)S(1)}, bf16[128,96]{0,1:T(8,128)(2,1)}, u32[]{:S(2)}) copy-start(bf16[128,96]{0,1:T(8,128)(2,1)} %param.21) | copy-start | bytes 73732
  89.2 75.3 %all-gather.10.cloned.1.call-start = ((), (), s32[]{:S(2)}) async-start(), calls=%async_computation.12 | async-start | bytes 2506752 | tf_op jit(solution)/shard_map/all_gather | solution.py:137
  90.2 146.4 %all-gather.8.cloned.1.call-start = ((), (), s32[]{:S(2)}) async-start(), calls=%async_computation.11 | async-start | bytes 2506752 | tf_op jit(solution)/shard_map/all_gather | solution.py:125
  121.3 247.5 %copy-start.30 = (bf16[128,96]{0,1:T(8,128)(2,1)}, bf16[128,96]{0,1:T(8,128)(2,1)S(1)}, u32[]{:S(2)}) copy-start(bf16[128,96]{0,1:T(8,128)(2,1)S(1)} %get-tuple-element.63) | copy-start | bytes 73732
  121.3 16.2 %copy-start.36 = (f32[3072]{0:T(1024)S(1)}, f32[3072]{0:T(1024)}, u32[]{:S(2)}) copy-start(f32[3072]{0:T(1024)} %param.22) | copy-start | bytes 36868
  121.5 22.8 %copy-start.11 = (bf16[8192,96]{0,1:T(8,128)(2,1)S(1)}, bf16[8192,96]{0,1:T(8,128)(2,1)}, u32[]{:S(2)}) copy-start(bf16[8192,96]{0,1:T(8,128)(2,1)} %all-gather.6.cloned.1.call-done) | copy-start | bytes 4718596
  134.6 11.2 %copy-start.3 = (bf16[32,20,96]{2,1,0:T(8,128)(2,1)}, bf16[32,20,96]{2,1,0:T(8,128)(2,1)S(1)}, u32[]{:S(2)}) copy-start(bf16[32,20,96]{2,1,0:T(8,128)(2,1)S(1)} %all_to_all.75) | copy-start | bytes 368644
  140.5 10.7 %all-to-all-start.3 = ((f32[32,128,1]{1,2,0:T(1,128)}), f32[32,128,1]{1,2,0:T(1,128)S(1)}, u32[]{:S(2)}, u32[]{:S(2)}) async-start(f32[32,128,1]{1,2,0:T(1,128)} %broadcast_in_dim.31), calls=%async_computation.3 | async-start | bytes 32768 | tf_op jit(solution)/shard_map/all_to_all | solution.py:26
  151.2 89.2 %all-to-all-start.2 = ((bf16[32,256,96]{1,2,0:T(8,128)(2,1)}), bf16[32,256,96]{1,2,0:T(8,128)(2,1)S(1)}, u32[]{:S(2)}, u32[]{:S(2)}) async-start(bf16[32,256,96]{1,2,0:T(8,128)(2,1)} %bitcast.172), calls=%async_computation.2 | async-start | bytes 3145728 | tf_op jit(solution)/shard_map/all_to_all | solution.py:124
  155.5 182.2 %reduce-scatter.2.cloned.1.call-start = ((), (), s32[]{:S(2)}) async-start(), calls=%async_computation.10 | async-start | bytes 4177920 | tf_op jit(solution)/shard_map/reduce_scatter | solution.py:34
  240.5 4.4 copy-start.1
  240.5 3.4 copy-start.10
  240.5 3.4 copy-start.15
  243.9 1.5 copy-start.9
  247.1 1.3 copy-start.16
  261.8 77.8 %copy-start.4 = (bf16[32,20,96]{2,1,0:T(8,128)(2,1)S(1)}, bf16[32,20,96]{2,1,0:T(8,128)(2,1)}, u32[]{:S(2)}) copy-start(bf16[32,20,96]{2,1,0:T(8,128)(2,1)} %copy-done.3) | copy-start | bytes 368644
  340.8 26.6 %all-to-all-start.5 = ((bf16[20,32,98]{2,0,1:T(8,128)(2,1)}), bf16[20,32,98]{2,0,1:T(8,128)(2,1)S(1)}, u32[]{:S(2)}, u32[]{:S(2)}) async-start(bf16[20,32,98]{2,0,1:T(8,128)(2,1)} %copy.203), calls=%async_computation.6 | async-start | bytes 393216 | tf_op jit(solution)/shard_map/all_to_all | solution.py:159
  367.4 0.7 copy-start.12
  368.1 21.0 %copy-start.2 = (bf16[32,256,96]{1,2,0:T(8,128)(2,1)S(1)}, bf16[32,256,96]{1,2,0:T(8,128)(2,1)}, u32[]{:S(2)}) copy-start(bf16[32,256,96]{1,2,0:T(8,128)(2,1)} %copy-done.1) | copy-start | bytes 4718596
  370.1 1.0 copy-start.33
  371.1 18.1 %all-to-all-start.6 = ((bf16[32,128,96]{1,2,0:T(8,128)(2,1)}), bf16[32,128,96]{1,2,0:T(8,128)(2,1)S(1)}, u32[]{:S(2)}, u32[]{:S(2)}) async-start(bf16[32,128,96]{1,2,0:T(8,128)(2,1)} %broadcast_in_dim.33), calls=%async_computation.7 | async-start | bytes 1572864 | tf_op jit(solution)/shard_map/all_to_all | solution.py:26
  389.1 0.9 copy-start.8
  389.2 0.9 copy-start.38
  389.2 1.0 copy-start.42
  389.2 1.0 copy-start.40
  389.2 1.1 copy-start.18
  389.2 1.3 copy-start.24
  389.2 4.2 copy-start.22
  389.2 4.3 copy-start.14
  389.9 4.5 copy-start.20
  390.0 14.3 %copy-start.29 = (bf16[2,128,128]{2,1,0:T(8,128)(2,1)S(1)}, bf16[2,128,128]{2,1,0:T(8,128)(2,1)}, u32[]{:S(2)}) copy-start(bf16[2,128,128]{2,1,0:T(8,128)(2,1)} %copy-done.28) | copy-start | bytes 196612
  390.1 26.6 %copy-start.19 = (bf16[128,256]{0,1:T(8,128)(2,1)S(1)}, bf16[128,256]{0,1:T(8,128)(2,1)}, u32[]{:S(2)}) copy-start(bf16[128,256]{0,1:T(8,128)(2,1)} %copy-done.17) | copy-start | bytes 196612
  390.3 46.7 %copy-start.6 = (f32[128,32,20]{0,1,2:T(8,128)S(1)}, f32[128,32,20]{0,1,2:T(8,128)}, u32[]{:S(2)}) copy-start(f32[128,32,20]{0,1,2:T(8,128)} %copy-done.5) | copy-start | bytes 983044
  390.3 46.7 %copy-start.31 = (bf16[128,96]{0,1:T(8,128)(2,1)S(1)}, bf16[128,96]{0,1:T(8,128)(2,1)}, u32[]{:S(2)}) copy-start(bf16[128,96]{0,1:T(8,128)(2,1)} %copy-done.30) | copy-start | bytes 73732
  390.7 9.1 %collective-permute-start.4 = (f32[2,128,128]{2,1,0:T(8,128)S(1)}, f32[2,128,128]{2,1,0:T(8,128)S(1)}, u32[]{:S(2)}, u32[]{:S(2)}) collective-permute-start(f32[2,128,128]{2,1,0:T(8,128)S(1)} %convolution_bitcast_fusion.4), channel_id=1, source_target_pairs={{0,32},{32,0},{64,96},{96,64},{128,160},{160,128},{192,224},{224,1... | collective-permute-start | bytes 393224 | tf_op jit(solution)/shard_map/ppermute | solution.py:14
  394.7 57.2 %copy-start.27 = (bf16[128,256]{1,0:T(8,128)(2,1)S(1)}, bf16[128,256]{1,0:T(8,128)(2,1)}, u32[]{:S(2)}) copy-start(bf16[128,256]{1,0:T(8,128)(2,1)} %param.16) | copy-start | bytes 196612
  395.4 57.5 %copy-start.25 = (bf16[128,256]{1,0:T(8,128)(2,1)S(1)}, bf16[128,256]{1,0:T(8,128)(2,1)}, u32[]{:S(2)}) copy-start(bf16[128,256]{1,0:T(8,128)(2,1)} %param.17) | copy-start | bytes 196612
  395.4 41.6 %all-to-all-start.7 = ((bf16[20,32,96]{2,0,1:T(8,128)(2,1)}), bf16[20,32,96]{2,0,1:T(8,128)(2,1)S(1)}, u32[]{:S(2)}, u32[]{:S(2)}) async-start(bf16[20,32,96]{2,0,1:T(8,128)(2,1)} %copy.207), calls=%async_computation.8 | async-start | bytes 393216 | tf_op jit(solution)/shard_map/all_to_all | solution.py:180
  399.9 10.6 %collective-permute-start.5 = (f32[2,128,128]{2,1,0:T(8,128)S(1)}, f32[2,128,128]{2,1,0:T(8,128)S(1)}, u32[]{:S(2)}, u32[]{:S(2)}) collective-permute-start(f32[2,128,128]{2,1,0:T(8,128)S(1)} %add.138), channel_id=1, source_target_pairs={{0,64},{32,96},{64,0},{96,32},{128,192},{160,224},{192,128},{224,1... | collective-permute-start | bytes 393224 | tf_op jit(solution)/shard_map/ppermute | solution.py:14
  410.6 17.9 %collective-permute-start.6 = (f32[2,128,128]{2,1,0:T(8,128)S(1)}, f32[2,128,128]{2,1,0:T(8,128)S(1)}, u32[]{:S(2)}, u32[]{:S(2)}) collective-permute-start(f32[2,128,128]{2,1,0:T(8,128)S(1)} %add.140), channel_id=1, source_target_pairs={{0,128},{32,160},{64,192},{96,224},{128,0},{160,32},{192,64},{224,... | collective-permute-start | bytes 393224 | tf_op jit(solution)/shard_map/ppermute | solution.py:14
  428.5 22.6 %collective-permute-start.7 = (f32[2,128,128]{2,1,0:T(8,128)S(1)}, f32[2,128,128]{2,1,0:T(8,128)S(1)}, u32[]{:S(2)}, u32[]{:S(2)}) collective-permute-start(f32[2,128,128]{2,1,0:T(8,128)S(1)} %add.142), channel_id=1, source_target_pairs={{0,256},{32,288},{64,320},{96,352},{128,384},{160,416},{192,448},{... | collective-permute-start | bytes 393224 | tf_op jit(solution)/shard_map/ppermute | solution.py:14
Sparse Core Ops, SparseCore 0:
  10.1 84.8 all-gather.5
  97.1 67.3 all-gather.9
  166.6 69.8 all-gather.7
  261.9 75.7 reduce-scatter.1
where the time goes:
time: 462 us; the launch traced here: 460 us
  waiting for transfers between devices  258 us (56%)
  starting transfers between devices  109 us (24%)
  local copies, waits for them, and re-layouts  35.1 us (8%)
  matrix products  19.3 us (4%)
  between operations  14.7 us (3%)
  blocking collectives  12.8 us (3%)
  other arithmetic  11.5 us (2%)
    reduce_scatter x1, waiting for transfers between devices, scatter_sum(): part = lax.psum_scatter(joined, axis, scatter_dimension=0, tiled=True)  75.8 us
    all_gather x1, waiting for transfers between devices, local(): portion = lax.all_gather(expert_in, 'ctx', axis=0, tiled=True)  68.1 us
    ppermute x8, starting transfers between devices, butterfly_sums(): other = lax.ppermute(total, axis, [(i, i ^ step) for i in range(count)])  50.9 us
    ppermute x8, waiting for transfers between devices, butterfly_sums(): other = lax.ppermute(total, axis, [(i, i ^ step) for i in range(count)])  49.4 us
    all_to_all x3, waiting for transfers between devices, gather_blocks(): return lax.all_to_all(spread, axis, 0, 0, tiled=True)  47.1 us
    all_to_all x3, starting transfers between devices, gather_blocks(): return lax.all_to_all(spread, axis, 0, 0, tiled=True)  22.2 us
    all_to_all x1, starting transfers between devices, local(): lax.all_to_all(payload, 'ep', split_axis=1, concat_axis=0, tiled=True)  18.3 us
    all_to_all x1, blocking collectives, local(): lax.all_to_all(picked.reshape(ep_count, capacity, columns), 'ep', 0, 0, t...  12.8 us
  transfers between devices with their start and end apart: 19, of which 12 were waited for; matrix products, arithmetic and copies ran while one was open for 7% of the time, Pallas kernels for 0%

commit v1 on v0

--- a/solution.py
+++ b/solution.py
@@ -122,7 +122,9 @@
     w_down = down_weight[0]
     hidden_block = w_gate.shape[0]
     w_rows = lax.all_to_all(w_blocks, "ep", 0, 0, tiled=True)
-    portion = lax.all_gather(expert_in, "ctx", axis=0, tiled=True)
+    portion = jnp.concatenate(
+        lax.all_to_all(jnp.stack([expert_in] * lax.axis_size("ctx")), "ctx", 0, 0), axis=0
+    )
     square_sums = jnp.sum(gather_blocks(jnp.sum(stream_f * stream_f, -1, keepdims=True), "ep"), 0)
     row_scale = lax.rsqrt(square_sums / model_width + 1e-05)
     projected = jnp.concatenate([contract_last(portion, w_gate), contract_last(portion, w_up)], 1)

time: 462 us -> 528 us (1.14)
  waiting for transfers between devices: 258 us -> 332 us
  blocking collectives: 12.8 us -> 0 us
    all_to_all x0 -> x2, waiting for transfers between devices: none -> 122 us  [the longest x1 115 us: local(): lax.all_to_all(jnp.stack([expert_in] * lax.axis_size('ctx')), 'ctx', 0, 0)]
    all_gather x1 -> x0, waiting for transfers between devices: 68.1 us -> none  [local(): portion = lax.all_gather(expert_in, 'ctx', axis=0, tiled=True)]
    ppermute x8, waiting for transfers between devices: 49.4 us -> 67.7 us  [butterfly_sums(): other = lax.ppermute(total, axis, [(i, i ^ step) for i in range(count)])]
    all_to_all x1 -> x0, blocking collectives: 12.8 us -> none  [local(): lax.all_to_all(picked.reshape(ep_count, capacity, columns), 'ep', 0, 0, t...]
    all_to_all x0 -> x2, starting transfers between devices: none -> 12.6 us  [the longest x1 7.33 us: local(): lax.all_to_all(jnp.stack([expert_in] * lax.axis_size('ctx')), 'ctx', 0, 0)]
    reduce_scatter x1, waiting for transfers between devices: 75.8 us -> 64.7 us  [scatter_sum(): part = lax.psum_scatter(joined, axis, scatter_dimension=0, tiled=True)]
    all_to_all x1, waiting for transfers between devices: 0.01 us -> 7.73 us  [local(): lax.all_to_all(grad_send, 'ep', split_axis=0, concat_axis=1, tiled=True)]
    all_to_all x3, starting transfers between devices: 22.2 us -> 15.6 us  [gather_blocks(): return lax.all_to_all(spread, axis, 0, 0, tiled=True)]
  transfers between devices with their start and end apart: 19 -> 20, of which waited for: 12 -> 18; matrix products, arithmetic and copies ran while one was open for 7% -> 5% of each run, Pallas kernels for 0% -> 0%
where the time goes in v1:
time: 528 us; the launch traced here: 526 us
  waiting for transfers between devices  332 us (63%)
  starting transfers between devices  114 us (22%)
  local copies, waits for them, and re-layouts  35.9 us (7%)
  matrix products  21.3 us (4%)
  between operations  14.8 us (3%)
  other arithmetic  8.24 us (2%)
    all_to_all x1, waiting for transfers between devices, local(): lax.all_to_all(jnp.stack([expert_in] * lax.axis_size('ctx')), 'ctx', 0, 0)  115 us
    ppermute x8, waiting for transfers between devices, butterfly_sums(): other = lax.ppermute(total, axis, [(i, i ^ step) for i in range(count)])  67.7 us
    reduce_scatter x1, waiting for transfers between devices, scatter_sum(): part = lax.psum_scatter(joined, axis, scatter_dimension=0, tiled=True)  64.7 us
    ppermute x8, starting transfers between devices, butterfly_sums(): other = lax.ppermute(total, axis, [(i, i ^ step) for i in range(count)])  53.3 us
    all_to_all x3, waiting for transfers between devices, gather_blocks(): return lax.all_to_all(spread, axis, 0, 0, tiled=True)  48.9 us
    all_to_all x1, starting transfers between devices, local(): lax.all_to_all(payload, 'ep', split_axis=1, concat_axis=0, tiled=True)  18.3 us
    all_to_all x3, starting transfers between devices, gather_blocks(): return lax.all_to_all(spread, axis, 0, 0, tiled=True)  15.6 us
  transfers between devices with their start and end apart: 20, of which 18 were waited for; matrix products, arithmetic and copies ran while one was open for 5% of the time, Pallas kernels for 0%

profile of v1, /device:TPU:1, one launch (start us, length us, event | category | flops | bytes accessed | tf_op | source)
XLA Modules:
  0.0 526.3 jit_solution(12627805411597208756)
XLA Ops:
  7.3 1.0 copy.262
  8.3 1.0 fusion.46
  9.3 4.4 collective-permute-start
  13.7 2.3 collective-permute-done
  16.1 5.6 %collective-permute-start.1 = (f32[2,128,128]{2,1,0:T(8,128)S(1)}, f32[2,128,128]{2,1,0:T(8,128)S(1)}, u32[]{:S(2)}, u32[]{:S(2)}) collective-permute-start(f32[2,128,128]{2,1,0:T(8,128)S(1)} %add.116), channel_id=1, source_target_pairs={{0,64},{32,96},{64,0},{96,32},{128,192},{160,224},{192,128},{224,1... | collective-permute-start | bytes 393224 | tf_op jit(solution)/shard_map/ppermute | solution.py:14
  21.8 1.0 copy.229
  22.8 2.7 collective-permute-done.1
  25.5 10.8 %collective-permute-start.2 = (f32[2,128,128]{2,1,0:T(8,128)S(1)}, f32[2,128,128]{2,1,0:T(8,128)S(1)}, u32[]{:S(2)}, u32[]{:S(2)}) collective-permute-start(f32[2,128,128]{2,1,0:T(8,128)S(1)} %add.118), channel_id=1, source_target_pairs={{0,128},{32,160},{64,192},{96,224},{128,0},{160,32},{192,64},{224,... | collective-permute-start | bytes 393224 | tf_op jit(solution)/shard_map/ppermute | solution.py:14
  36.3 1.1 fusion.14
  37.4 9.6 %collective-permute-done.2 = f32[2,128,128]{2,1,0:T(8,128)S(1)} collective-permute-done((f32[2,128,128]{2,1,0:T(8,128)S(1)}, f32[2,128,128]{2,1,0:T(8,128)S(1)}, u32[]{:S(2)}, u32[]{:S(2)}) %collective-permute-start.2) | collective-permute-done | bytes 131104 | tf_op jit(solution)/shard_map/ppermute | solution.py:14
  47.0 15.2 %collective-permute-start.3 = (f32[2,128,128]{2,1,0:T(8,128)S(1)}, f32[2,128,128]{2,1,0:T(8,128)S(1)}, u32[]{:S(2)}, u32[]{:S(2)}) collective-permute-start(f32[2,128,128]{2,1,0:T(8,128)S(1)} %add.120), channel_id=1, source_target_pairs={{0,256},{32,288},{64,320},{96,352},{128,384},{160,416},{192,448},{... | collective-permute-start | bytes 393224 | tf_op jit(solution)/shard_map/ppermute | solution.py:14
  62.5 14.7 %collective-permute-done.3 = f32[2,128,128]{2,1,0:T(8,128)S(1)} collective-permute-done((f32[2,128,128]{2,1,0:T(8,128)S(1)}, f32[2,128,128]{2,1,0:T(8,128)S(1)}, u32[]{:S(2)}, u32[]{:S(2)}) %collective-permute-start.3) | collective-permute-done | bytes 131104 | tf_op jit(solution)/shard_map/ppermute | solution.py:14
  78.5 1.6 broadcast_in_dim.30
  80.1 7.8 %all-to-all-start = ((bf16[32,128,256]{2,1,0:T(8,128)(2,1)}), bf16[32,128,256]{2,1,0:T(8,128)(2,1)}, u32[]{:S(2)}, u32[]{:S(2)}) async-start(bf16[32,128,256]{2,1,0:T(8,128)(2,1)} %broadcast_in_dim.30), calls=%async_computation | async-start | bytes 4194304 | tf_op jit(solution)/shard_map/all_to_all | solution.py:26
  88.8 27.9 %all-to-all-done = bf16[32,128,256]{2,1,0:T(8,128)(2,1)} async-done(((bf16[32,128,256]{2,1,0:T(8,128)(2,1)}), bf16[32,128,256]{2,1,0:T(8,128)(2,1)}, u32[]{:S(2)}, u32[]{:S(2)}) %all-to-all-start) | async-done | bytes 2097184 | tf_op jit(solution)/shard_map/all_to_all | solution.py:26
  116.7 2.9 fusion.50
  120.7 5.3 %all-to-all-start.1 = ((bf16[32,20,96]{2,1,0:T(8,128)(2,1)}), bf16[32,20,96]{2,1,0:T(8,128)(2,1)S(1)}, u32[]{:S(2)}, u32[]{:S(2)}) async-start(bf16[32,20,96]{2,1,0:T(8,128)(2,1)} %reshape.195), calls=%async_computation.1 | async-start | bytes 393216 | tf_op jit(solution)/shard_map/all_to_all | solution.py:116
  126.5 0.8 all_to_all.60
  127.3 7.1 %all-to-all-done.1 = bf16[32,20,96]{2,1,0:T(8,128)(2,1)S(1)} async-done(((bf16[32,20,96]{2,1,0:T(8,128)(2,1)}), bf16[32,20,96]{2,1,0:T(8,128)(2,1)S(1)}, u32[]{:S(2)}, u32[]{:S(2)}) %all-to-all-start.1) | async-done | bytes 122912 | tf_op jit(solution)/shard_map/all_to_all | solution.py:116
  134.3 3.8 all-to-all-start.5
  138.7 7.7 %all-to-all-done.5 = bf16[32,20,96]{2,1,0:T(8,128)(2,1)S(1)} async-done(((bf16[32,20,96]{2,1,0:T(8,128)(2,1)}), bf16[32,20,96]{2,1,0:T(8,128)(2,1)S(1)}, u32[]{:S(2)}, u32[]{:S(2)}) %all-to-all-start.5) | async-done | bytes 122912 | tf_op jit(solution)/shard_map/all_to_all | solution.py:138
  147.1 3.8 all-to-all-start.4
  151.0 6.8 %all-to-all-done.4 = f32[32,128,1]{1,2,0:T(1,128)S(1)} async-done(((f32[32,128,1]{1,2,0:T(1,128)}), f32[32,128,1]{1,2,0:T(1,128)S(1)}, u32[]{:S(2)}, u32[]{:S(2)}) %all-to-all-start.4) | async-done | bytes 16416 | tf_op jit(solution)/shard_map/all_to_all | solution.py:26
  157.8 1.7 stack.2
  159.5 7.3 %all-to-all-start.2 = ((bf16[16,20,3072]{2,1,0:T(8,128)(2,1)}), bf16[16,20,3072]{2,1,0:T(8,128)(2,1)S(1)}, u32[]{:S(2)}, u32[]{:S(2)}) async-start(bf16[16,20,3072]{2,1,0:T(8,128)(2,1)} %stack.2), calls=%async_computation.2 | async-start | bytes 4718592 | tf_op jit(solution)/shard_map/all_to_all | solution.py:126
  166.8 1.6 copy.200
  168.5 1.8 reshape.207
  170.3 2.8 copy.265
  173.1 114.9 %all-to-all-done.2 = bf16[16,20,3072]{2,1,0:T(8,128)(2,1)S(1)} async-done(((bf16[16,20,3072]{2,1,0:T(8,128)(2,1)}), bf16[16,20,3072]{2,1,0:T(8,128)(2,1)S(1)}, u32[]{:S(2)}, u32[]{:S(2)}) %all-to-all-start.2) | async-done | bytes 1966112 | tf_op jit(solution)/shard_map/all_to_all | solution.py:126
  288.0 5.9 %all-to-all-start.3 = ((bf16[32,256,96]{1,2,0:T(8,128)(2,1)}), bf16[32,256,96]{1,2,0:T(8,128)(2,1)}, u32[]{:S(2)}, u32[]{:S(2)}) async-start(bf16[32,256,96]{1,2,0:T(8,128)(2,1)} %bitcast.170), calls=%async_computation.3 | async-start | bytes 3145728 | tf_op jit(solution)/shard_map/all_to_all | solution.py:124
  294.7 7.1 %all-gather.6.cloned.1.call-done = bf16[16,20,3072]{2,1,0:T(8,128)(2,1)} async-done(((bf16[1,20,3072]{2,1,0:T(8,128)(2,1)}), bf16[16,20,3072]{2,1,0:T(8,128)(2,1)}) %all-gather.6.cloned.1.call-update) | async-done | bytes 1966096 | tf_op jit(solution)/shard_map/all_gather | solution.py:139
  301.8 4.0 reshape.208
  305.8 2.0 reshape.196
  307.8 2.8 fusion.9
  310.6 5.8 %all-to-all-done.3 = bf16[32,256,96]{1,2,0:T(8,128)(2,1)} async-done(((bf16[32,256,96]{1,2,0:T(8,128)(2,1)}), bf16[32,256,96]{1,2,0:T(8,128)(2,1)}, u32[]{:S(2)}, u32[]{:S(2)}) %all-to-all-start.3) | async-done | bytes 1572896 | tf_op jit(solution)/shard_map/all_to_all | solution.py:124
  316.3 2.8 fusion.5
  319.2 0.9 fusion.1
  321.4 0.8 fusion.7
  322.6 2.0 fusion
  324.7 4.0 reshape.199
  328.6 2.2 reshape.197
  330.8 5.2 pad_maximum_fusion
  336.9 64.7 %reduce-scatter.2.cloned.1.call-done = bf16[1,40,3072]{2,1,0:T(8,128)(2,1)} async-done(((bf16[16,40,3072]{2,1,0:T(8,128)(2,1)}), bf16[1,40,3072]{2,1,0:T(8,128)(2,1)}) %reduce-scatter.2.cloned.1.call-update) | async-done | bytes 245776 | tf_op jit(solution)/shard_map/reduce_scatter | solution.py:34
  401.6 1.0 fusion.64
  403.4 0.8 copy.203
  404.1 18.3 %all-to-all-start.6 = ((bf16[20,32,98]{2,0,1:T(8,128)(2,1)}), bf16[20,32,98]{2,0,1:T(8,128)(2,1)S(1)}, u32[]{:S(2)}, u32[]{:S(2)}) async-start(bf16[20,32,98]{2,0,1:T(8,128)(2,1)} %copy.203), calls=%async_computation.7 | async-start | bytes 393216 | tf_op jit(solution)/shard_map/all_to_all | solution.py:161
  422.5 8.2 %all-to-all-done.6 = bf16[20,32,98]{2,0,1:T(8,128)(2,1)S(1)} async-done(((bf16[20,32,98]{2,0,1:T(8,128)(2,1)}), bf16[20,32,98]{2,0,1:T(8,128)(2,1)S(1)}, u32[]{:S(2)}, u32[]{:S(2)}) %all-to-all-start.6) | async-done | bytes 125472 | tf_op jit(solution)/shard_map/all_to_all | solution.py:161
  431.9 1.0 broadcast_in_dim.33
  432.9 3.9 all-to-all-start.7
  436.9 14.2 %all-to-all-done.7 = bf16[32,128,96]{1,2,0:T(8,128)(2,1)S(1)} async-done(((bf16[32,128,96]{1,2,0:T(8,128)(2,1)}), bf16[32,128,96]{1,2,0:T(8,128)(2,1)S(1)}, u32[]{:S(2)}, u32[]{:S(2)}) %all-to-all-start.7) | async-done | bytes 786464 | tf_op jit(solution)/shard_map/all_to_all | solution.py:26
  451.1 2.1 fusion.66
  454.1 0.8 copy.207
  454.9 4.0 all-to-all-start.8
  459.1 2.3 collective-permute-start.4
  461.7 0.7 copy.217
  462.4 3.3 collective-permute-done.4
  465.7 3.6 collective-permute-start.5
  469.5 7.1 %collective-permute-done.5 = f32[2,128,128]{2,1,0:T(8,128)S(1)} collective-permute-done((f32[2,128,128]{2,1,0:T(8,128)S(1)}, f32[2,128,128]{2,1,0:T(8,128)S(1)}, u32[]{:S(2)}, u32[]{:S(2)}) %collective-permute-start.5) | collective-permute-done | bytes 131104 | tf_op jit(solution)/shard_map/ppermute | solution.py:14
  476.6 5.0 collective-permute-start.6
  481.7 13.5 %collective-permute-done.6 = f32[2,128,128]{2,1,0:T(8,128)S(1)} collective-permute-done((f32[2,128,128]{2,1,0:T(8,128)S(1)}, f32[2,128,128]{2,1,0:T(8,128)S(1)}, u32[]{:S(2)}, u32[]{:S(2)}) %collective-permute-start.6) | collective-permute-done | bytes 131104 | tf_op jit(solution)/shard_map/ppermute | solution.py:14
  495.2 6.3 %collective-permute-start.7 = (f32[2,128,128]{2,1,0:T(8,128)S(1)}, f32[2,128,128]{2,1,0:T(8,128)S(1)}, u32[]{:S(2)}, u32[]{:S(2)}) collective-permute-start(f32[2,128,128]{2,1,0:T(8,128)S(1)} %add.142), channel_id=1, source_target_pairs={{0,256},{32,288},{64,320},{96,352},{128,384},{160,416},{192,448},{... | collective-permute-start | bytes 393224 | tf_op jit(solution)/shard_map/ppermute | solution.py:14
  501.5 1.0 fusion.26
  502.5 14.5 %collective-permute-done.7 = f32[2,128,128]{2,1,0:T(8,128)S(1)} collective-permute-done((f32[2,128,128]{2,1,0:T(8,128)S(1)}, f32[2,128,128]{2,1,0:T(8,128)S(1)}, u32[]{:S(2)}, u32[]{:S(2)}) %collective-permute-start.7) | collective-permute-done | bytes 131104 | tf_op jit(solution)/shard_map/ppermute | solution.py:14
  517.9 0.7 copy.218
  (164 shorter events, 13.9 us)
Async XLA Ops:
  7.2 312.0 %copy-start = (bf16[1,192,3072]{2,1,0:T(8,128)(2,1)S(1)}, bf16[1,192,3072]{2,1,0:T(8,128)(2,1)}, u32[]{:S(2)}) copy-start(bf16[1,192,3072]{2,1,0:T(8,128)(2,1)} %param.28) | copy-start | bytes 3538948
  7.2 55.1 %copy-start.19 = (bf16[128,256]{1,0:T(8,128)(2,1)S(1)}, bf16[128,256]{1,0:T(8,128)(2,1)}, u32[]{:S(2)}) copy-start(bf16[128,256]{1,0:T(8,128)(2,1)} %param.17) | copy-start | bytes 196612
  7.2 70.1 %copy-start.26 = (f32[2,128,128]{2,1,0:T(8,128)S(1)}, f32[2,128,128]{2,1,0:T(8,128)}, u32[]{:S(2)}) copy-start(f32[2,128,128]{2,1,0:T(8,128)} %param.18) | copy-start | bytes 393220
  7.2 71.1 %copy-start.34 = (f32[256]{0:T(256)S(1)}, f32[256]{0:T(256)}, u32[]{:S(2)}) copy-start(f32[256]{0:T(256)} %param.19) | copy-start | bytes 3076
  7.2 109.5 %all-gather.4.cloned.1.call-start = ((), (), s32[]{:S(2)}) async-start(), calls=%async_computation.10 | async-start | bytes 1671168 | tf_op jit(solution)/shard_map/all_gather | solution.py:77
  8.3 13.4 %copy-start.17 = (bf16[128,256]{0,1:T(8,128)(2,1)}, bf16[128,256]{0,1:T(8,128)(2,1)S(1)}, u32[]{:S(2)}) copy-start(bf16[128,256]{0,1:T(8,128)(2,1)S(1)} %copy.262) | copy-start | bytes 196612
  9.3 6.7 %collective-permute-start = (f32[2,128,128]{2,1,0:T(8,128)S(1)}, f32[2,128,128]{2,1,0:T(8,128)S(1)}, u32[]{:S(2)}, u32[]{:S(2)}) collective-permute-start(f32[2,128,128]{2,1,0:T(8,128)S(1)} %fusion.46), channel_id=1, source_target_pairs={{0,32},{32,0},{64,96},{96,64},{128,160},{160,128},{192,224},{224,1... | collective-permute-start | bytes 393224 | tf_op jit(solution)/shard_map/ppermute | solution.py:14
  16.1 9.4 %collective-permute-start.1 = (f32[2,128,128]{2,1,0:T(8,128)S(1)}, f32[2,128,128]{2,1,0:T(8,128)S(1)}, u32[]{:S(2)}, u32[]{:S(2)}) collective-permute-start(f32[2,128,128]{2,1,0:T(8,128)S(1)} %add.116), channel_id=1, source_target_pairs={{0,64},{32,96},{64,0},{96,32},{128,192},{160,224},{192,128},{224,1... | collective-permute-start | bytes 393224 | tf_op jit(solution)/shard_map/ppermute | solution.py:14
  22.7 57.4 %copy-start.14 = (bf16[128,256]{0,1:T(8,128)(2,1)}, bf16[128,256]{0,1:T(8,128)(2,1)S(1)}, u32[]{:S(2)}) copy-start(bf16[128,256]{0,1:T(8,128)(2,1)S(1)} %copy.229) | copy-start | bytes 196612
  22.8 39.8 %copy-start.32 = (pred[128,128]{1,0:T(8,128)(4,1)}, pred[128,128]{1,0:T(8,128)(4,1)S(1)}, u32[]{:S(2)}) copy-start(pred[128,128]{1,0:T(8,128)(4,1)S(1)} %iota_compare_fusion) | copy-start | bytes 49156
  25.5 21.5 %collective-permute-start.2 = (f32[2,128,128]{2,1,0:T(8,128)S(1)}, f32[2,128,128]{2,1,0:T(8,128)S(1)}, u32[]{:S(2)}, u32[]{:S(2)}) collective-permute-start(f32[2,128,128]{2,1,0:T(8,128)S(1)} %add.118), channel_id=1, source_target_pairs={{0,128},{32,160},{64,192},{96,224},{128,0},{160,32},{192,64},{224,... | collective-permute-start | bytes 393224 | tf_op jit(solution)/shard_map/ppermute | solution.py:14
  37.4 25.1 %copy-start.22 = (bf16[2,128,128]{2,1,0:T(8,128)(2,1)}, bf16[2,128,128]{2,1,0:T(8,128)(2,1)S(1)}, u32[]{:S(2)}) copy-start(bf16[2,128,128]{2,1,0:T(8,128)(2,1)S(1)} %fusion.14) | copy-start | bytes 196612
  47.0 30.2 %collective-permute-start.3 = (f32[2,128,128]{2,1,0:T(8,128)S(1)}, f32[2,128,128]{2,1,0:T(8,128)S(1)}, u32[]{:S(2)}, u32[]{:S(2)}) collective-permute-start(f32[2,128,128]{2,1,0:T(8,128)S(1)} %add.120), channel_id=1, source_target_pairs={{0,256},{32,288},{64,320},{96,352},{128,384},{160,416},{192,448},{... | collective-permute-start | bytes 393224 | tf_op jit(solution)/shard_map/ppermute | solution.py:14
  77.3 1.1 copy-start.10
  77.7 0.8 copy-start.38
  77.7 0.8 copy-start.36
  80.1 7.9 %copy-start.41 = (s32[128,2]{0,1:T(2,128)S(1)}, s32[128,2]{0,1:T(2,128)}, u32[]{:S(2)}) copy-start(s32[128,2]{0,1:T(2,128)} %param.24) | copy-start | bytes 3076
  80.1 7.9 %copy-start.42 = (s32[128,2]{0,1:T(2,128)S(1)}, s32[128,2]{0,1:T(2,128)}, u32[]{:S(2)}) copy-start(s32[128,2]{0,1:T(2,128)} %param.23) | copy-start | bytes 3076
  80.1 8.0 %copy-start.40 = (f32[128,2]{0,1:T(2,128)S(1)}, f32[128,2]{0,1:T(2,128)}, u32[]{:S(2)}) copy-start(f32[128,2]{0,1:T(2,128)} %param.25) | copy-start | bytes 3076
  80.1 36.6 %all-to-all-start = ((bf16[32,128,256]{2,1,0:T(8,128)(2,1)}), bf16[32,128,256]{2,1,0:T(8,128)(2,1)}, u32[]{:S(2)}, u32[]{:S(2)}) async-start(bf16[32,128,256]{2,1,0:T(8,128)(2,1)} %broadcast_in_dim.30), calls=%async_computation | async-start | bytes 4194304 | tf_op jit(solution)/shard_map/all_to_all | solution.py:26
  88.0 28.7 %copy-start.44 = (bf16[128,96]{0,1:T(8,128)(2,1)S(1)}, bf16[128,96]{0,1:T(8,128)(2,1)}, u32[]{:S(2)}) copy-start(bf16[128,96]{0,1:T(8,128)(2,1)} %param.21) | copy-start | bytes 73732
  88.3 31.3 %copy-start.5 = (f32[128,32,20]{0,1,2:T(8,128)}, f32[128,32,20]{0,1,2:T(8,128)S(1)}, u32[]{:S(2)}) copy-start(f32[128,32,20]{0,1,2:T(8,128)S(1)} %get-tuple-element.53) | copy-start | bytes 983044
  88.5 31.1 %copy-start.1 = (f32[128,640]{0,1:T(8,128)}, f32[128,640]{0,1:T(8,128)S(1)}, u32[]{:S(2)}) copy-start(f32[128,640]{0,1:T(8,128)S(1)} %reshape.194) | copy-start | bytes 983044
  116.7 9.3 %copy-start.28 = (bf16[128,96]{0,1:T(8,128)(2,1)S(1)}, bf16[128,96]{0,1:T(8,128)(2,1)}, u32[]{:S(2)}) copy-start(bf16[128,96]{0,1:T(8,128)(2,1)} %param.29) | copy-start | bytes 73732
  119.6 18.6 %copy-start.24 = (bf16[128,96]{0,1:T(8,128)(2,1)}, bf16[128,96]{0,1:T(8,128)(2,1)S(1)}, u32[]{:S(2)}) copy-start(bf16[128,96]{0,1:T(8,128)(2,1)S(1)} %get-tuple-element.63) | copy-start | bytes 73732
  120.7 30.2 %copy-start.30 = (f32[3072]{0:T(1024)S(1)}, f32[3072]{0:T(1024)}, u32[]{:S(2)}) copy-start(f32[3072]{0:T(1024)} %param.22) | copy-start | bytes 36868
  120.7 13.6 %all-to-all-start.1 = ((bf16[32,20,96]{2,1,0:T(8,128)(2,1)}), bf16[32,20,96]{2,1,0:T(8,128)(2,1)S(1)}, u32[]{:S(2)}, u32[]{:S(2)}) async-start(bf16[32,20,96]{2,1,0:T(8,128)(2,1)} %reshape.195), calls=%async_computation.1 | async-start | bytes 393216 | tf_op jit(solution)/shard_map/all_to_all | solution.py:116
  134.3 25.1 %copy-start.3 = (bf16[32,20,96]{2,1,0:T(8,128)(2,1)}, bf16[32,20,96]{2,1,0:T(8,128)(2,1)S(1)}, u32[]{:S(2)}) copy-start(bf16[32,20,96]{2,1,0:T(8,128)(2,1)S(1)} %all-to-all-done.1) | copy-start | bytes 368644
  134.3 12.1 %all-to-all-start.5 = ((bf16[32,20,96]{2,1,0:T(8,128)(2,1)}), bf16[32,20,96]{2,1,0:T(8,128)(2,1)S(1)}, u32[]{:S(2)}, u32[]{:S(2)}) async-start(bf16[32,20,96]{2,1,0:T(8,128)(2,1)} %all_to_all.60), calls=%async_computation.5 | async-start | bytes 393216 | tf_op jit(solution)/shard_map/all_to_all | solution.py:138
  146.4 13.1 %copy-start.16 = (bf16[32,20,96]{2,1,0:T(8,128)(2,1)}, bf16[32,20,96]{2,1,0:T(8,128)(2,1)S(1)}, u32[]{:S(2)}) copy-start(bf16[32,20,96]{2,1,0:T(8,128)(2,1)S(1)} %all-to-all-done.5) | copy-start | bytes 368644
  147.1 10.7 %all-to-all-start.4 = ((f32[32,128,1]{1,2,0:T(1,128)}), f32[32,128,1]{1,2,0:T(1,128)S(1)}, u32[]{:S(2)}, u32[]{:S(2)}) async-start(f32[32,128,1]{1,2,0:T(1,128)} %broadcast_in_dim.31), calls=%async_computation.4 | async-start | bytes 32768 | tf_op jit(solution)/shard_map/all_to_all | solution.py:26
  159.5 128.6 %all-to-all-start.2 = ((bf16[16,20,3072]{2,1,0:T(8,128)(2,1)}), bf16[16,20,3072]{2,1,0:T(8,128)(2,1)S(1)}, u32[]{:S(2)}, u32[]{:S(2)}) async-start(bf16[16,20,3072]{2,1,0:T(8,128)(2,1)} %stack.2), calls=%async_computation.2 | async-start | bytes 4718592 | tf_op jit(solution)/shard_map/all_to_all | solution.py:126
  166.8 135.0 %all-gather.6.cloned.1.call-start = ((), (), s32[]{:S(2)}) async-start(), calls=%async_computation.12 | async-start | bytes 2506752 | tf_op jit(solution)/shard_map/all_gather | solution.py:139
  288.0 28.3 %all-to-all-start.3 = ((bf16[32,256,96]{1,2,0:T(8,128)(2,1)}), bf16[32,256,96]{1,2,0:T(8,128)(2,1)}, u32[]{:S(2)}, u32[]{:S(2)}) async-start(bf16[32,256,96]{1,2,0:T(8,128)(2,1)} %bitcast.170), calls=%async_computation.3 | async-start | bytes 3145728 | tf_op jit(solution)/shard_map/all_to_all | solution.py:124
  293.9 107.7 %reduce-scatter.2.cloned.1.call-start = ((), (), s32[]{:S(2)}) async-start(), calls=%async_computation.11 | async-start | bytes 4177920 | tf_op jit(solution)/shard_map/reduce_scatter | solution.py:34
  310.6 8.6 %copy-start.9 = (bf16[320,3072]{1,0:T(8,128)(2,1)S(1)}, bf16[320,3072]{1,0:T(8,128)(2,1)}, u32[]{:S(2)}) copy-start(bf16[320,3072]{1,0:T(8,128)(2,1)} %reshape.208) | copy-start | bytes 5898244
  320.1 1.3 copy-start.12
  321.4 1.3 copy-start.13
  336.0 0.7 copy-start.31
  336.0 66.8 %copy-start.4 = (bf16[32,20,96]{2,1,0:T(8,128)(2,1)S(1)}, bf16[32,20,96]{2,1,0:T(8,128)(2,1)}, u32[]{:S(2)}) copy-start(bf16[32,20,96]{2,1,0:T(8,128)(2,1)} %copy-done.3) | copy-start | bytes 368644
  336.7 85.7 %copy-start.43 = (f32[128]{0:T(128)S(1)}, f32[128]{0:T(128)}, u32[]{:S(2)}) copy-start(f32[128]{0:T(128)} %reduce_sum.89) | copy-start | bytes 1540
  402.7 28.5 %copy-start.2 = (f32[128,640]{0,1:T(8,128)S(1)}, f32[128,640]{0,1:T(8,128)}, u32[]{:S(2)}) copy-start(f32[128,640]{0,1:T(8,128)} %copy-done.1) | copy-start | bytes 983044
  402.7 28.8 %copy-start.25 = (bf16[128,96]{0,1:T(8,128)(2,1)S(1)}, bf16[128,96]{0,1:T(8,128)(2,1)}, u32[]{:S(2)}) copy-start(bf16[128,96]{0,1:T(8,128)(2,1)} %copy-done.24) | copy-start | bytes 73732
  402.7 28.8 %copy-start.29 = (bf16[128,96]{0,1:T(8,128)(2,1)S(1)}, bf16[128,96]{0,1:T(8,128)(2,1)}, u32[]{:S(2)}) copy-start(bf16[128,96]{0,1:T(8,128)(2,1)} %param.29) | copy-start | bytes 73732
  404.1 26.6 %all-to-all-start.6 = ((bf16[20,32,98]{2,0,1:T(8,128)(2,1)}), bf16[20,32,98]{2,0,1:T(8,128)(2,1)S(1)}, u32[]{:S(2)}, u32[]{:S(2)}) async-start(bf16[20,32,98]{2,0,1:T(8,128)(2,1)} %copy.203), calls=%async_computation.7 | async-start | bytes 393216 | tf_op jit(solution)/shard_map/all_to_all | solution.py:161
  431.8 21.4 %copy-start.27 = (bf16[128,96]{0,1:T(8,128)(2,1)}, bf16[128,96]{0,1:T(8,128)(2,1)S(1)}, u32[]{:S(2)}) copy-start(bf16[128,96]{0,1:T(8,128)(2,1)S(1)} %fusion.25) | copy-start | bytes 73732
  432.9 20.4 %copy-start.8 = (f32[128,2,128]{0,2,1:T(8,128)S(1)}, f32[128,2,128]{0,2,1:T(8,128)}, u32[]{:S(2)}) copy-start(f32[128,2,128]{0,2,1:T(8,128)} %copy-done.7) | copy-start | bytes 393220
  432.9 20.4 %copy-start.35 = (f32[256]{0:T(256)S(1)}, f32[256]{0:T(256)}, u32[]{:S(2)}) copy-start(f32[256]{0:T(256)} %param.19) | copy-start | bytes 3076
  432.9 20.5 %copy-start.39 = (f32[128,2]{0,1:T(2,128)S(1)}, f32[128,2]{0,1:T(2,128)}, u32[]{:S(2)}) copy-start(f32[128,2]{0,1:T(2,128)} %copy-done.38) | copy-start | bytes 3076
  432.9 20.6 %copy-start.37 = (f32[128,2]{0,1:T(2,128)S(1)}, f32[128,2]{0,1:T(2,128)}, u32[]{:S(2)}) copy-start(f32[128,2]{0,1:T(2,128)} %copy-done.36) | copy-start | bytes 3076
  432.9 20.7 %copy-start.15 = (bf16[128,256]{0,1:T(8,128)(2,1)S(1)}, bf16[128,256]{0,1:T(8,128)(2,1)}, u32[]{:S(2)}) copy-start(bf16[128,256]{0,1:T(8,128)(2,1)} %copy-done.14) | copy-start | bytes 196612
  432.9 18.2 %all-to-all-start.7 = ((bf16[32,128,96]{1,2,0:T(8,128)(2,1)}), bf16[32,128,96]{1,2,0:T(8,128)(2,1)S(1)}, u32[]{:S(2)}, u32[]{:S(2)}) async-start(bf16[32,128,96]{1,2,0:T(8,128)(2,1)} %broadcast_in_dim.33), calls=%async_computation.8 | async-start | bytes 1572864 | tf_op jit(solution)/shard_map/all_to_all | solution.py:26
  436.8 16.9 %copy-start.20 = (bf16[128,256]{1,0:T(8,128)(2,1)S(1)}, bf16[128,256]{1,0:T(8,128)(2,1)}, u32[]{:S(2)}) copy-start(bf16[128,256]{1,0:T(8,128)(2,1)} %param.17) | copy-start | bytes 196612
  436.9 16.9 %copy-start.33 = (pred[128,128]{1,0:T(8,128)(4,1)S(1)}, pred[128,128]{1,0:T(8,128)(4,1)}, u32[]{:S(2)}) copy-start(pred[128,128]{1,0:T(8,128)(4,1)} %copy-done.32) | copy-start | bytes 49156
  436.9 22.1 %copy-start.18 = (bf16[128,256]{0,1:T(8,128)(2,1)S(1)}, bf16[128,256]{0,1:T(8,128)(2,1)}, u32[]{:S(2)}) copy-start(bf16[128,256]{0,1:T(8,128)(2,1)} %copy-done.17) | copy-start | bytes 196612
  436.9 24.6 %copy-start.11 = (f32[2,128,128]{2,1,0:T(8,128)S(1)}, f32[2,128,128]{2,1,0:T(8,128)}, u32[]{:S(2)}) copy-start(f32[2,128,128]{2,1,0:T(8,128)} %copy-done.10) | copy-start | bytes 393220
  453.3 28.3 %copy-start.23 = (bf16[2,128,128]{2,1,0:T(8,128)(2,1)S(1)}, bf16[2,128,128]{2,1,0:T(8,128)(2,1)}, u32[]{:S(2)}) copy-start(bf16[2,128,128]{2,1,0:T(8,128)(2,1)} %copy-done.22) | copy-start | bytes 196612
  453.6 48.0 %copy-start.6 = (f32[128,32,20]{0,1,2:T(8,128)S(1)}, f32[128,32,20]{0,1,2:T(8,128)}, u32[]{:S(2)}) copy-start(f32[128,32,20]{0,1,2:T(8,128)} %copy-done.5) | copy-start | bytes 983044
  454.9 46.6 %all-to-all-start.8 = ((bf16[20,32,96]{2,0,1:T(8,128)(2,1)}), bf16[20,32,96]{2,0,1:T(8,128)(2,1)S(1)}, u32[]{:S(2)}, u32[]{:S(2)}) async-start(bf16[20,32,96]{2,0,1:T(8,128)(2,1)} %copy.207), calls=%async_computation.9 | async-start | bytes 393216 | tf_op jit(solution)/shard_map/all_to_all | solution.py:182
  459.1 6.6 %collective-permute-start.4 = (f32[2,128,128]{2,1,0:T(8,128)S(1)}, f32[2,128,128]{2,1,0:T(8,128)S(1)}, u32[]{:S(2)}, u32[]{:S(2)}) collective-permute-start(f32[2,128,128]{2,1,0:T(8,128)S(1)} %convolution_bitcast_fusion.4), channel_id=1, source_target_pairs={{0,32},{32,0},{64,96},{96,64},{128,160},{160,128},{192,224},{224,1... | collective-permute-start | bytes 393224 | tf_op jit(solution)/shard_map/ppermute | solution.py:14
  461.7 57.0 %copy-start.21 = (bf16[128,256]{1,0:T(8,128)(2,1)S(1)}, bf16[128,256]{1,0:T(8,128)(2,1)}, u32[]{:S(2)}) copy-start(bf16[128,256]{1,0:T(8,128)(2,1)} %param.16) | copy-start | bytes 196612
  465.7 10.8 %collective-permute-start.5 = (f32[2,128,128]{2,1,0:T(8,128)S(1)}, f32[2,128,128]{2,1,0:T(8,128)S(1)}, u32[]{:S(2)}, u32[]{:S(2)}) collective-permute-start(f32[2,128,128]{2,1,0:T(8,128)S(1)} %add.138), channel_id=1, source_target_pairs={{0,64},{32,96},{64,0},{96,32},{128,192},{160,224},{192,128},{224,1... | collective-permute-start | bytes 393224 | tf_op jit(solution)/shard_map/ppermute | solution.py:14
  476.6 18.6 %collective-permute-start.6 = (f32[2,128,128]{2,1,0:T(8,128)S(1)}, f32[2,128,128]{2,1,0:T(8,128)S(1)}, u32[]{:S(2)}, u32[]{:S(2)}) collective-permute-start(f32[2,128,128]{2,1,0:T(8,128)S(1)} %add.140), channel_id=1, source_target_pairs={{0,128},{32,160},{64,192},{96,224},{128,0},{160,32},{192,64},{224,... | collective-permute-start | bytes 393224 | tf_op jit(solution)/shard_map/ppermute | solution.py:14
  495.2 21.8 %collective-permute-start.7 = (f32[2,128,128]{2,1,0:T(8,128)S(1)}, f32[2,128,128]{2,1,0:T(8,128)S(1)}, u32[]{:S(2)}, u32[]{:S(2)}) collective-permute-start(f32[2,128,128]{2,1,0:T(8,128)S(1)} %add.142), channel_id=1, source_target_pairs={{0,256},{32,288},{64,320},{96,352},{128,384},{160,416},{192,448},{... | collective-permute-start | bytes 393224 | tf_op jit(solution)/shard_map/ppermute | solution.py:14
  (1 other events, 0.7 us)
Sparse Core Ops, SparseCore 0:
  21.9 76.1 all-gather.3
  170.4 131.3 all-gather.5
  336.2 65.4 reduce-scatter.1
